TPU v7x, 512 devices: a whole 4x8x8 slice. The times are simulated.
512 devices in a mesh: page: 32 (over y_lo, z), req: 16 (over y_hi, x, core).
Axes of the slice: x: 4, y: 8 (y_hi: 2, y_lo: 4; y = y_hi * 4 + y_lo), z: 8, core: 2. Of those that a mesh axis runs over, the one named last changes fastest.
Arguments:
- queries: bfloat16 [256, 8192], P('req'), may hold values from -250 to 250
- key_pool: bfloat16 [512, 128, 1024], P(('page', 'req')), may hold values from -6 to 6
- value_pool: bfloat16 [512, 128, 1024], P(('page', 'req')), may hold values from -6 to 6
- page_table: int32 [256, 32], P('req'), may hold values from 0 to 511, as said below
- page_count: int32 [256], P('req'), may hold values from 1 to 32, as said below
Outputs:
- attended: bfloat16 [256, 8192], P('req', 'page')
Inputs may be any that keep to these rules, and one draw needn't show every extreme that they name: `page_table`: rows of a request's table up to page_count are distinct pages; slots beyond it hold 0 and are not part of the context. `page_count`: some request has 32 live slots and some has one.
All inputs are finite; a program needn't handle non-finite values.
Results may differ from a plain program's by a relative error of at most 0.013.
Values may be sent and summed in bfloat16 or wider, within the bound.
No kernel may reach another device: no remote copies, remote signals or barrier semaphores. Data moves between devices by JAX's collectives and lax.ppermute only.
A program may use at most 64 MiB of HBM per device.

v0:
```python
import math
import jax
import jax.numpy as jnp
from jax import lax
from jax.sharding import Mesh
from jax.sharding import PartitionSpec as P

H = 64
KVH = 8
HD = 128
LANES = 128


def split_pair(value):
    high = lax.reduce_precision(value, exponent_bits=8, mantissa_bits=7)
    low = lax.reduce_precision(value - high, exponent_bits=8, mantissa_bits=7)
    return (high, low)


def body(queries, key_pool, value_pool, page_table, page_count):
    n_page = lax.axis_size("page")
    n_yh = lax.axis_size("yh")
    n_xc = lax.axis_size("xc")
    page_index = lax.axis_index("page")
    yh_index = lax.axis_index("yh")
    pages_held = key_pool.shape[0]
    page_len = key_pool.shape[1]
    per_kv = H // KVH
    own_heads = H // n_page
    rows = queries.shape[0]
    score_scale = 1.0 / math.sqrt(HD)
    row_pages = n_yh * n_xc * pages_held
    row_ids = page_index * row_pages + jnp.arange(row_pages, dtype=jnp.int32)
    slot_live = jnp.arange(page_table.shape[1], dtype=jnp.int32)[None, :] < page_count[:, None]
    row_hit = jnp.any(
        (page_table[:, :, None] == row_ids[None, None, :]) & slot_live[:, :, None], axis=1
    )
    mask_cols = -(-row_pages // LANES) * LANES
    row_hit = jnp.pad(row_hit.astype(queries.dtype), ((0, 0), (0, mask_cols - row_pages)))
    packed = jnp.concatenate([queries, row_hit], axis=1)
    all_packed = lax.all_gather(packed, "yh", tiled=True)
    keys = lax.all_gather(key_pool, "xc", tiled=True)
    values = lax.all_to_all(
        jnp.broadcast_to(value_pool[None], (n_xc,) + value_pool.shape).reshape(
            (n_xc * pages_held,) + value_pool.shape[1:]
        ),
        "xc",
        0,
        0,
        tiled=True,
    )
    req_rows = all_packed.shape[0]
    all_q = all_packed[:, : H * HD]
    held = n_xc * pages_held
    page_hit = lax.dynamic_slice_in_dim(all_packed, H * HD + yh_index * held, held, 1) > 0.5
    token_hit = jnp.repeat(page_hit, page_len, axis=1)[:, None, None, :]
    grouped = all_q.reshape(req_rows, KVH, per_kv, HD)
    token_keys = keys.reshape(-1, KVH, HD)
    token_values = values.reshape(-1, KVH, HD)
    scores = (
        jnp.einsum("rkgd,tkd->rkgt", grouped, token_keys, preferred_element_type=jnp.float32)
        * score_scale
    )
    scores = jnp.where(token_hit, scores, jnp.float32(-1e30))
    max_hi, max_lo = split_pair(jnp.max(scores, axis=3))
    local_max = max_hi + max_lo
    exp_terms = jnp.where(token_hit, jnp.exp(scores - local_max[..., None]), jnp.float32(0.0))
    local_sum = jnp.sum(exp_terms, axis=3)
    weights = exp_terms.astype(jnp.bfloat16)
    local_out = jnp.einsum(
        "rkgt,tkd->rkgd", weights, token_values, preferred_element_type=jnp.float32
    )
    n_blocks = n_page * n_yh
    block_rows = rows * own_heads
    out_blocks = local_out.astype(jnp.bfloat16)
    out_blocks = out_blocks.reshape(n_yh, rows, n_page, own_heads, HD).transpose(2, 0, 1, 3, 4)
    out_blocks = out_blocks.reshape(n_blocks, block_rows, HD)
    sum_hi, sum_lo = split_pair(local_sum)

    def to_blocks(stat):
        stat = (
            stat.astype(jnp.bfloat16).reshape(n_yh, rows, n_page, own_heads).transpose(2, 0, 1, 3)
        )
        return stat.reshape(n_blocks, block_rows)

    stat_cols = -(-4 * block_rows // HD) * HD
    stats = jnp.concatenate(
        [to_blocks(max_hi), to_blocks(max_lo), to_blocks(sum_hi), to_blocks(sum_lo)]
        + [jnp.zeros((n_blocks, stat_cols - 4 * block_rows), jnp.bfloat16)],
        axis=1,
    )
    payload = jnp.concatenate([out_blocks, stats.reshape(n_blocks, -1, HD)], axis=1)
    arrived = lax.all_to_all(payload, ("page", "yh"), 0, 0, tiled=True)
    part_out = arrived[:, :block_rows, :].astype(jnp.float32)
    part_stats = arrived[:, block_rows:, :].reshape(n_blocks, stat_cols).astype(jnp.float32)
    part_max = part_stats[:, :block_rows] + part_stats[:, block_rows : 2 * block_rows]
    part_sum = (
        part_stats[:, 2 * block_rows : 3 * block_rows]
        + part_stats[:, 3 * block_rows : 4 * block_rows]
    )
    joint_max = jnp.max(part_max, axis=0)
    factor = jnp.exp(part_max - joint_max[None, :])
    joint_sum = jnp.sum(part_sum * factor, axis=0)
    joint_out = jnp.sum(part_out * factor[..., None], axis=0)
    result = joint_out / joint_sum[:, None]
    return result.reshape(rows, own_heads * HD).astype(jnp.bfloat16)


def solution(mesh):
    n_page, n_req = mesh.devices.shape
    n_yh = 2 if n_req % 2 == 0 else 1
    split = Mesh(mesh.devices.reshape(n_page, n_yh, n_req // n_yh), ("page", "yh", "xc"))
    req = ("yh", "xc")
    return jax.shard_map(
        body,
        mesh=split,
        in_specs=(
            P(req, None),
            P(("page",) + req, None, None),
            P(("page",) + req, None, None),
            P(req, None),
            P(req),
        ),
        out_specs=P(req, "page"),
        check_vma=False,
    )
```

profile of v0, /device:TPU:64, one launch (start us, length us, event | category | flops | bytes accessed | tf_op | source)
XLA Modules:
  0.0 122.1 jit_solution(18207185544669441702)
XLA Ops:
  6.5 0.7 all-gather.2.cloned.1.call-update
  7.3 2.5 %reshape.90 = bf16[8,128,1024]{2,1,0:T(8,128)(2,1)} broadcast(bf16[128,1024]{1,0:T(8,128)(2,1)} %bitcast.89), dimensions={1,2} | broadcast | bytes 2359296 | tf_op jit(solution)/shard_map/reshape | solution.py:44
  9.8 4.3 %all-to-all-start = ((bf16[8,128,1024]{2,1,0:T(8,128)(2,1)}), bf16[8,128,1024]{2,1,0:T(8,128)(2,1)S(1)}, u32[]{:S(2)}, u32[]{:S(2)}) async-start(bf16[8,128,1024]{2,1,0:T(8,128)(2,1)} %reshape.90), calls=%async_computation | async-start | bytes 4194304 | tf_op jit(solution)/shard_map/all_to_all | solution.py:43
  14.1 0.7 iota_compare_fusion
  14.8 1.1 and_reduce_fusion
  15.9 1.0 pad_maximum_fusion.1
  16.9 15.4 %all_gather.6 = bf16[32,8320]{1,0:T(8,128)(2,1)S(1)} all-gather(bf16[16,8320]{1,0:T(8,128)(2,1)S(1)} %pad_maximum_fusion.1), channel_id=1, replica_groups=mesh['page'=32,'yh'=2,'xc'=8] {'yh'}, dimensions={0}, use_global_device_ids=true | all-gather | bytes 798720 | tf_op jit(solution)/shard_map/all_gather | solution.py:41
  32.4 0.1 broadcast_in_dim.40
  32.5 0.1 copy.69
  32.7 17.0 %all-to-all-done = bf16[8,128,1024]{2,1,0:T(8,128)(2,1)S(1)} async-done(((bf16[8,128,1024]{2,1,0:T(8,128)(2,1)}), bf16[8,128,1024]{2,1,0:T(8,128)(2,1)S(1)}, u32[]{:S(2)}, u32[]{:S(2)}) %all-to-all-start) | async-done | bytes 2097184 | tf_op jit(solution)/shard_map/all_to_all | solution.py:43
  49.7 2.0 %copy.71 = bf16[128,8,8,128]{3,2,1,0:T(8,128)(2,1)} copy(bf16[128,8,8,128]{3,1,2,0:T(8,128)(2,1)S(1)} %bitcast.78) | data formatting | bytes 4194304
  51.7 2.2 %copy.70 = bf16[128,8,8,128]{3,2,1,0:T(8,128)(2,1)S(1)} copy(bf16[128,8,8,128]{3,1,2,0:T(8,128)(2,1)} %bitcast.81) | data formatting | bytes 4194304
  53.9 5.1 %bitcast_reduce_fusion = (f32[32,8,8]{2,0,1:T(8,128)S(1)}, f32[8,32,8,1024]{3,2,1,0:T(8,128)}) fusion(pred[32,1024]{1,0:T(8,128)(4,1)S(1)} %bitcast.86, bf16[1024,8,128,1]{2,1,0,3:T(8,128)(2,1)S(1)} %bitcast.77, bf16[32,8,8,128]{3,2,1,0:T(8,128)(2,1)S(1)} %bitcast.79), kind=kOutput, calls=%fused_computation.1 | convolution fusion | flops 543160320 | bytes 11051008 | tf_op jit(solution)/shard_map/rkgd,tkd->rkgt/dot_general | solution.py:61
  59.1 0.1 reduce_max.21
  59.3 5.3 %fusion.2 = f32[32,8,8]{2,0,1:T(8,128)S(1)} fusion(f32[8,32,8,1024]{3,2,1,0:T(8,128)} %get-tuple-element.12, f32[32,8,8]{2,0,1:T(8,128)S(1)} %copy.48, pred[32,1024]{1,0:T(8,128)(4,1)S(1)} %bitcast.87), kind=kLoop, calls=%fused_computation.5 | loop fusion | flops 10483712 | bytes 8437760 | tf_op jit(solution)/shard_map/reduce_sum | solution.py:68
  64.7 0.1 reduce_sum.32
  64.9 0.6 copy.56
  65.5 0.3 reshape.96
  65.9 0.6 copy.57
  66.5 0.3 reshape.97
  66.9 0.6 copy.53
  67.5 0.3 reshape.94
  67.8 0.6 copy.54
  68.5 0.3 reshape.95
  68.8 0.1 copy.59
  68.9 5.9 %fusion.16 = bf16[32,8,8,128]{3,2,0,1:T(8,128)(2,1)S(1)} fusion(bf16[1024,8,128,1]{2,1,0,3:T(8,128)(2,1)S(1)} %bitcast.82, f32[8,32,8,1024]{3,2,1,0:T(8,128)} %get-tuple-element.12, f32[32,8,8]{2,0,1:T(8,128)S(1)} %copy.48, pred[32,1024]{1,0:T(8,128)(4,1)S(1)} %bitcast.88), kind=kOutput, calls=%fused_computation.14 | convolution fusion | flops 547618816 | bytes 11051008 | tf_op jit(solution)/shard_map/rkgt,tkd->rkgd/dot_general | solution.py:70
  74.9 0.5 copy.51
  75.5 38.4 %all_to_all.10 = bf16[64,33,128]{2,1,0:T(8,128)(2,1)S(1)} all-to-all(bf16[64,33,128]{2,1,0:T(8,128)(2,1)S(1)} %pad_maximum_fusion), channel_id=1, replica_groups=mesh['page'=32,'yh'=2,'xc'=8] {'page','yh'}, dimensions={0} | all-to-all | bytes 1081344 | tf_op jit(solution)/shard_map/all_to_all | solution.py:93
  113.9 0.1 fusion.34
  114.0 0.1 fusion.30
  114.2 0.3 multiply_reduce_fusion
  114.7 0.6 fusion.33
  (22 shorter events, 0.9 us)
Async XLA Ops:
  6.5 45.1 %all-gather.2.cloned.1.call-start = ((), (), s32[]{:S(2)}) async-start(), calls=%async_computation.2 | async-start | bytes 2359296 | tf_op jit(solution)/shard_map/all_gather | solution.py:42
  9.8 39.9 %all-to-all-start = ((bf16[8,128,1024]{2,1,0:T(8,128)(2,1)}), bf16[8,128,1024]{2,1,0:T(8,128)(2,1)S(1)}, u32[]{:S(2)}, u32[]{:S(2)}) async-start(bf16[8,128,1024]{2,1,0:T(8,128)(2,1)} %reshape.90), calls=%async_computation | async-start | bytes 4194304 | tf_op jit(solution)/shard_map/all_to_all | solution.py:43
  59.0 9.9 %copy-start = (bf16[128,8,8,128]{3,2,1,0:T(8,128)(2,1)S(1)}, bf16[128,8,8,128]{3,2,1,0:T(8,128)(2,1)}, u32[]{:S(2)}) copy-start(bf16[128,8,8,128]{3,2,1,0:T(8,128)(2,1)} %copy.71) | copy-start | bytes 6291460
Sparse Core Ops, SparseCore 0:
  9.5 40.7 all-gather.1
where the time goes:
time: 123 us; the launch traced here: 122 us
  blocking collectives  53.8 us (44%)
  waiting for transfers between devices  17.7 us (14%)
  between operations  13.6 us (11%)
  local copies, waits for them, and re-layouts  12.1 us (10%)
  matrix products  11 us (9%)
  other arithmetic  9.6 us (8%)
  starting transfers between devices  4.3 us (3%)
    all_to_all x1, blocking collectives, body(): arrived = lax.all_to_all(payload, ('page', 'yh'), 0, 0, tiled=True)  38.4 us
    all_to_all x1, waiting for transfers between devices, body(): lax.all_to_all(jnp.broadcast_to(value_pool[None], (n_xc,) + value_pool.sh...  17 us
    all_gather x1, blocking collectives, body(): all_packed = lax.all_gather(packed, 'yh', tiled=True)  15.4 us
    dot_general x1, matrix products, body(): jnp.einsum('rkgt,tkd->rkgd', weights, token_values, preferred_element_typ...  5.88 us
    reduce_sum x1, other arithmetic, body(): local_sum = jnp.sum(exp_terms, axis=3)  5.32 us
    dot_general x1, matrix products, body(): jnp.einsum('rkgd,tkd->rkgt', grouped, token_keys, preferred_element_type=...  5.13 us
    unnamed x7, local copies, waits for them, and re-layouts  4.4 us
    all_to_all x1, starting transfers between devices, body(): lax.all_to_all(jnp.broadcast_to(value_pool[None], (n_xc,) + value_pool.sh...  4.3 us
  transfers between devices with their start and end apart: 2, of which 1 were waited for; matrix products, arithmetic and copies ran while one was open for 6% of the time, Pallas kernels for 0%

commit v1 on v0

--- a/solution.py
+++ b/solution.py
@@ -38,7 +38,9 @@
     mask_cols = -(-row_pages // LANES) * LANES
     row_hit = jnp.pad(row_hit.astype(queries.dtype), ((0, 0), (0, mask_cols - row_pages)))
     packed = jnp.concatenate([queries, row_hit], axis=1)
-    all_packed = lax.all_gather(packed, "yh", tiled=True)
+    all_packed = jnp.concatenate(
+        lax.all_to_all(jnp.stack([packed] * lax.axis_size("yh")), "yh", 0, 0), axis=0
+    )
     keys = lax.all_gather(key_pool, "xc", tiled=True)
     values = lax.all_to_all(
         jnp.broadcast_to(value_pool[None], (n_xc,) + value_pool.shape).reshape(

time: 123 us -> 136 us (1.11)
  waiting for transfers between devices: 17.7 us -> 27.5 us
  blocking collectives: 53.8 us -> 57.8 us
    all_to_all x0 -> x1, blocking collectives: none -> 23 us  [body(): lax.all_to_all(jnp.stack([packed] * lax.axis_size('yh')), 'yh', 0, 0)]
    all_gather x1 -> x0, blocking collectives: 15.4 us -> none  [body(): all_packed = lax.all_gather(packed, 'yh', tiled=True)]
    all_to_all x1, waiting for transfers between devices: 17 us -> 26.8 us  [body(): lax.all_to_all(jnp.broadcast_to(value_pool[None], (n_xc,) + value_pool.sh...]
    all_to_all x1, blocking collectives: 38.4 us -> 34.8 us  [body(): arrived = lax.all_to_all(payload, ('page', 'yh'), 0, 0, tiled=True)]
where the time goes in v1:
time: 136 us
  blocking collectives  57.8 us (42%)
  waiting for transfers between devices  27.5 us (20%)
  between operations  13.6 us (10%)
  local copies, waits for them, and re-layouts  12.1 us (9%)
  matrix products  11 us (8%)
  other arithmetic  9.65 us (7%)
  starting transfers between devices  4.3 us (3%)
    all_to_all x1, blocking collectives, body(): arrived = lax.all_to_all(payload, ('page', 'yh'), 0, 0, tiled=True)  34.8 us
    all_to_all x1, waiting for transfers between devices, body(): lax.all_to_all(jnp.broadcast_to(value_pool[None], (n_xc,) + value_pool.sh...  26.8 us
    all_to_all x1, blocking collectives, body(): lax.all_to_all(jnp.stack([packed] * lax.axis_size('yh')), 'yh', 0, 0)  23 us
    dot_general x1, matrix products, body(): jnp.einsum('rkgt,tkd->rkgd', weights, token_values, preferred_element_typ...  5.9 us
    reduce_sum x1, other arithmetic, body(): local_sum = jnp.sum(exp_terms, axis=3)  5.33 us
    dot_general x1, matrix products, body(): jnp.einsum('rkgd,tkd->rkgt', grouped, token_keys, preferred_element_type=...  5.13 us
    unnamed x7, local copies, waits for them, and re-layouts  4.4 us
    all_to_all x1, starting transfers between devices, body(): lax.all_to_all(jnp.broadcast_to(value_pool[None], (n_xc,) + value_pool.sh...  4.3 us
  transfers between devices with their start and end apart: 2, of which 1 were waited for; matrix products, arithmetic and copies ran while one was open for 6% of the time, Pallas kernels for 0%

profile of v1, /device:TPU:64, one launch (start us, length us, event | category | flops | bytes accessed | tf_op | source)
XLA Modules:
  0.0 136.1 jit_solution(3449780425088390809)
XLA Ops:
  6.5 0.7 all-gather.2.cloned.1.call-update
  7.3 0.7 iota_compare_fusion
  8.0 1.1 and_reduce_fusion
  9.1 1.0 maximum_bitcast_fusion
  10.2 23.0 %all_to_all.15 = bf16[2,16,8320]{2,1,0:T(8,128)(2,1)S(1)} all-to-all(bf16[2,16,8320]{2,1,0:T(8,128)(2,1)S(1)} %pad_maximum_fusion.1), channel_id=1, replica_groups=mesh['page'=32,'yh'=2,'xc'=8] {'yh'}, dimensions={0} | all-to-all | bytes 1064960 | tf_op jit(solution)/shard_map/all_to_all | solution.py:42
  33.2 2.5 %reshape.94 = bf16[8,128,1024]{2,1,0:T(8,128)(2,1)} broadcast(bf16[128,1024]{1,0:T(8,128)(2,1)} %bitcast.94), dimensions={1,2} | broadcast | bytes 2359296 | tf_op jit(solution)/shard_map/reshape | solution.py:46
  35.7 4.3 %all-to-all-start.1 = ((bf16[8,128,1024]{2,1,0:T(8,128)(2,1)}), bf16[8,128,1024]{2,1,0:T(8,128)(2,1)S(1)}, u32[]{:S(2)}, u32[]{:S(2)}) async-start(bf16[8,128,1024]{2,1,0:T(8,128)(2,1)} %reshape.94), calls=%async_computation.1 | async-start | bytes 4194304 | tf_op jit(solution)/shard_map/all_to_all | solution.py:45
  40.0 0.1 broadcast_in_dim.40
  40.2 0.1 copy.69
  40.3 26.8 %all-to-all-done.1 = bf16[8,128,1024]{2,1,0:T(8,128)(2,1)S(1)} async-done(((bf16[8,128,1024]{2,1,0:T(8,128)(2,1)}), bf16[8,128,1024]{2,1,0:T(8,128)(2,1)S(1)}, u32[]{:S(2)}, u32[]{:S(2)}) %all-to-all-start.1) | async-done | bytes 2097184 | tf_op jit(solution)/shard_map/all_to_all | solution.py:45
  67.1 2.0 %copy.71 = bf16[128,8,8,128]{3,2,1,0:T(8,128)(2,1)} copy(bf16[128,8,8,128]{3,1,2,0:T(8,128)(2,1)S(1)} %bitcast.81) | data formatting | bytes 4194304
  69.1 2.2 %copy.70 = bf16[128,8,8,128]{3,2,1,0:T(8,128)(2,1)S(1)} copy(bf16[128,8,8,128]{3,1,2,0:T(8,128)(2,1)} %bitcast.86) | data formatting | bytes 4194304
  71.4 5.1 %bitcast_reduce_fusion = (f32[32,8,8]{2,0,1:T(8,128)S(1)}, f32[8,32,8,1024]{3,2,1,0:T(8,128)}) fusion(pred[32,1024]{1,0:T(8,128)(4,1)S(1)} %bitcast.91, bf16[1024,8,128,1]{2,1,0,3:T(8,128)(2,1)S(1)} %bitcast.80, bf16[32,8,8,128]{3,2,1,0:T(8,128)(2,1)S(1)} %bitcast.82), kind=kOutput, calls=%fused_computation.1 | convolution fusion | flops 543160320 | bytes 11051008 | tf_op jit(solution)/shard_map/rkgd,tkd->rkgt/dot_general | solution.py:63
  76.6 0.1 reduce_max.21
  76.8 5.3 %fusion.2 = f32[32,8,8]{2,0,1:T(8,128)S(1)} fusion(f32[8,32,8,1024]{3,2,1,0:T(8,128)} %get-tuple-element.12, f32[32,8,8]{2,0,1:T(8,128)S(1)} %copy.48, pred[32,1024]{1,0:T(8,128)(4,1)S(1)} %bitcast.92), kind=kLoop, calls=%fused_computation.5 | loop fusion | flops 10483712 | bytes 8437760 | tf_op jit(solution)/shard_map/reduce_sum | solution.py:70
  82.2 0.1 reduce_sum.32
  82.4 0.6 copy.56
  83.0 0.3 reshape.100
  83.4 0.6 copy.57
  84.0 0.3 reshape.101
  84.4 0.6 copy.53
  85.0 0.3 reshape.98
  85.3 0.6 copy.54
  85.9 0.3 reshape.99
  86.3 0.1 copy.59
  86.4 5.9 %fusion.16 = bf16[32,8,8,128]{3,2,0,1:T(8,128)(2,1)S(1)} fusion(bf16[1024,8,128,1]{2,1,0,3:T(8,128)(2,1)S(1)} %bitcast.87, f32[8,32,8,1024]{3,2,1,0:T(8,128)} %get-tuple-element.12, f32[32,8,8]{2,0,1:T(8,128)S(1)} %copy.48, pred[32,1024]{1,0:T(8,128)(4,1)S(1)} %bitcast.93), kind=kOutput, calls=%fused_computation.14 | convolution fusion | flops 547618816 | bytes 11051008 | tf_op jit(solution)/shard_map/rkgt,tkd->rkgd/dot_general | solution.py:72
  92.4 0.5 copy.51
  93.0 34.8 %all_to_all.16 = bf16[64,33,128]{2,1,0:T(8,128)(2,1)S(1)} all-to-all(bf16[64,33,128]{2,1,0:T(8,128)(2,1)S(1)} %pad_maximum_fusion), channel_id=1, replica_groups=mesh['page'=32,'yh'=2,'xc'=8] {'page','yh'}, dimensions={0} | all-to-all | bytes 1081344 | tf_op jit(solution)/shard_map/all_to_all | solution.py:95
  127.9 0.1 fusion.34
  128.0 0.1 fusion.30
  128.1 0.3 multiply_reduce_fusion
  128.6 0.6 fusion.33
  (23 shorter events, 0.9 us)
Async XLA Ops:
  6.5 62.6 %all-gather.2.cloned.1.call-start = ((), (), s32[]{:S(2)}) async-start(), calls=%async_computation.3 | async-start | bytes 2359296 | tf_op jit(solution)/shard_map/all_gather | solution.py:44
  35.7 31.5 %all-to-all-start.1 = ((bf16[8,128,1024]{2,1,0:T(8,128)(2,1)}), bf16[8,128,1024]{2,1,0:T(8,128)(2,1)S(1)}, u32[]{:S(2)}, u32[]{:S(2)}) async-start(bf16[8,128,1024]{2,1,0:T(8,128)(2,1)} %reshape.94), calls=%async_computation.1 | async-start | bytes 4194304 | tf_op jit(solution)/shard_map/all_to_all | solution.py:45
  76.5 9.9 %copy-start = (bf16[128,8,8,128]{3,2,1,0:T(8,128)(2,1)S(1)}, bf16[128,8,8,128]{3,2,1,0:T(8,128)(2,1)}, u32[]{:S(2)}) copy-start(bf16[128,8,8,128]{3,2,1,0:T(8,128)(2,1)} %copy.71) | copy-start | bytes 6291460
Sparse Core Ops, SparseCore 0:
  9.5 34.5 all-gather.1
